TPU v7x, 128 devices: a whole 4x4x4 slice. The times are simulated.
128 devices in a mesh: dp: 8 (over z, core), ctx: 16 (over y, x).
Axes of the slice: x: 4, y: 4, z: 4, core: 2. Of those that a mesh axis runs over, the one named last changes fastest.
Arguments:
- ids: int32 [8, 4096, 8], P('dp', 'ctx'), may hold values from 0 to 1023
- tables: bfloat16 [8, 1024, 1024], P(None, 'dp', 'ctx'), may hold values from -2.09375 to 2.09375
- w_qkv: bfloat16 [1024, 3072], P('dp'), may hold values from -5 to 5
- w_out: bfloat16 [1024, 1024], P('dp'), may hold values from -0.1875 to 0.1875
- attn_gain: float32 [1024], replicated, may hold values from 0.1 to 1.9
- conv_gain: float32 [1024], replicated, may hold values from 0.1 to 1.9
- conv_kernel: float32 [31, 1024], replicated, may hold values from -1 to 1
- back_list: int32 [16, 2], replicated, may hold values from 0 to 17, as said below
- ahead_list: int32 [16, 1], replicated, may hold values from 1 to 17, as said below
- cotangent: bfloat16 [8, 4096, 1024], P('dp', 'ctx'), may hold values from -8 to 8
Outputs:
- block_out: bfloat16 [8, 4096, 1024], P('dp', 'ctx')
- grad_embedded: bfloat16 [8, 4096, 1024], P('dp', 'ctx')
- grad_qkv: float32 [1024, 3072], P('dp')
- grad_out: float32 [1024, 1024], P('dp')
- grad_kernel: float32 [31, 1024], replicated
Inputs may be any that keep to these rules, and one draw needn't show every extreme that they name: `back_list`: row b lists distinct blocks among b - 2 .. b - 1 that exist, first, then the filler 16 + 1; block 2 and the last block list all 2, the first none. `ahead_list`: row b lists distinct blocks among b + 1 .. b + 1 that exist, first, then the filler 16 + 1; block 0 lists all 1, the last none.
All inputs are finite; a program needn't handle non-finite values.
Results may differ from a plain program's by a relative error of at most 0.015.
Values may be sent and summed in bfloat16 or wider, within the bound.
No kernel may reach another device: no remote copies, remote signals or barrier semaphores. Data moves between devices by JAX's collectives and lax.ppermute only.
A program may use at most 128 MiB of HBM per device.

v0:
```python
import jax
import jax.numpy as jnp
from jax import lax
from jax.sharding import PartitionSpec as P

HEADS = 16
EPSILON = 1e-06
NEGATIVE = -1e30


def from_behind(value, axis, steps):
    count = lax.axis_size(axis)
    first, last = (max(0, -steps), min(count, count - steps))
    return lax.ppermute(value, axis, [(source, source + steps) for source in range(first, last)])


def with_halo(block, sides, width):
    for axis, dim in sides:
        count = lax.axis_size(axis)
        forward = [(i, i + 1) for i in range(count - 1)]
        backward = [(target, source) for source, target in forward]
        low = lax.ppermute(
            lax.slice_in_dim(block, block.shape[dim] - width, None, axis=dim), axis, forward
        )
        high = lax.ppermute(lax.slice_in_dim(block, 0, width, axis=dim), axis, backward)
        block = jnp.concatenate([low, block, high], axis=dim)
    return block


def inverse_rms(features):
    return lax.rsqrt(jnp.mean(features * features, axis=-1, keepdims=True) + EPSILON)


def norm_back(features, inverse, gains, upstream):
    inner = jnp.mean(features * gains * upstream, axis=-1, keepdims=True)
    return inverse * gains * upstream - features * inverse * inverse * inverse * inner


def silu_slope(conv_sum):
    sigmoid = jax.nn.sigmoid(conv_sum)
    return sigmoid * (1.0 + conv_sum * (1.0 - sigmoid))


def block_scores(queries, key_block, listed_block, score_scale):
    return jnp.where(
        listed_block,
        jnp.einsum("rqhd,rkhd->rhqk", queries, key_block, preferred_element_type=jnp.float32)
        * score_scale,
        NEGATIVE,
    )


def probabilities(queries, key_part, listed, score_scale):
    pieces = [
        block_scores(queries, key_part[:, position], listed[position], score_scale)
        for position in range(key_part.shape[1])
    ]
    scores = jnp.concatenate(pieces, axis=3)
    highest = jnp.max(scores, axis=3, keepdims=True)
    weights = jnp.exp(scores - highest)
    return weights / jnp.sum(weights, axis=3, keepdims=True)


def on_device(
    ids, tables, w_qkv, w_out, attn_gain, conv_gain, conv_kernel, back_list, ahead_list, cotangent
):
    recordings = ids.shape[0]
    frames_dev = ids.shape[1]
    head_count = HEADS
    tap_count = conv_kernel.shape[0]
    rim_width = (tap_count - 1) // 2
    group_width = 4
    group_count = head_count // group_width
    ids_whole = lax.all_gather(ids, "ctx", axis=1, tiled=True)
    table_whole = lax.all_gather(tables, "dp", axis=1, tiled=True)
    columns = jnp.zeros(ids_whole.shape[:2] + (table_whole.shape[2],), jnp.float32)
    for codebook in range(table_whole.shape[0]):
        columns = columns + jnp.take(
            table_whole[codebook], ids_whole[:, :, codebook], axis=0
        ).astype(jnp.float32)
    embedded = lax.all_to_all(
        columns.astype(jnp.bfloat16), "ctx", split_axis=1, concat_axis=2, tiled=True
    )
    weight_qkv, weight_out = (
        lax.all_gather(w_qkv, "dp", axis=0, tiled=True),
        lax.all_gather(w_out, "dp", axis=0, tiled=True),
    )
    model_width = weight_out.shape[0]
    head_size = model_width // head_count
    score_scale = head_size ** (-0.5)
    features = embedded.astype(jnp.float32).reshape(-1, model_width)
    attn_inverse = inverse_rms(features)
    normed = (features * attn_inverse * attn_gain).astype(jnp.bfloat16)
    projected = jnp.dot(normed, weight_qkv, preferred_element_type=jnp.float32).astype(jnp.bfloat16)
    projected = projected.reshape(recordings, frames_dev, 3 * model_width)
    own_pairs = projected[:, :, model_width:]
    ctx_index = lax.axis_index("ctx")
    back_row = lax.dynamic_index_in_dim(back_list, ctx_index, 0, keepdims=False)
    ahead_row = lax.dynamic_index_in_dim(ahead_list, ctx_index, 0, keepdims=False)
    offsets = [-(step + 1) for step in range(back_list.shape[1])] + [1]
    listed_items = [jnp.array(True)]
    pair_blocks = [own_pairs]
    for offset in offsets:
        list_row = back_row if offset < 0 else ahead_row
        listed_items.append(jnp.any(list_row == ctx_index + offset))
        pair_blocks.append(from_behind(own_pairs, "ctx", -offset))
    listed = jnp.stack(listed_items)
    seen_count = len(pair_blocks)
    stacked = jnp.stack(pair_blocks, axis=1)
    key_all = stacked[..., :model_width].reshape(
        recordings, seen_count, frames_dev, head_count, head_size
    )
    value_all = stacked[..., model_width:].reshape(
        recordings, seen_count, frames_dev, head_count, head_size
    )
    query_all = projected[:, :, :model_width].reshape(recordings, frames_dev, head_count, head_size)

    def forward_group(group):
        first_head = group * group_width
        queries = lax.dynamic_slice_in_dim(query_all, first_head, group_width, 2)
        key_part = lax.dynamic_slice_in_dim(key_all, first_head, group_width, 3)
        value_part = lax.dynamic_slice_in_dim(value_all, first_head, group_width, 3)
        probs_low = probabilities(queries, key_part, listed, score_scale).astype(jnp.bfloat16)
        value_flat = value_part.reshape(recordings, -1, group_width, head_size)
        return jnp.einsum(
            "rhqk,rkhd->rqhd", probs_low, value_flat, preferred_element_type=jnp.float32
        ).astype(jnp.bfloat16)

    mixed = lax.map(forward_group, jnp.arange(group_count, dtype=jnp.int32))
    mixed = jnp.moveaxis(mixed, 0, 2).reshape(recordings * frames_dev, model_width)
    projection = jnp.dot(mixed, weight_out, preferred_element_type=jnp.float32)
    middle = (features + projection).astype(jnp.bfloat16)
    middle_wide = middle.astype(jnp.float32)
    conv_inverse = inverse_rms(middle_wide)
    conv_input = (
        (middle_wide * conv_inverse * conv_gain)
        .astype(jnp.bfloat16)
        .reshape(recordings, frames_dev, model_width)
    )
    padded = with_halo(conv_input, (("ctx", 1),), rim_width).astype(jnp.float32)
    conv_sum = jnp.zeros((recordings, frames_dev, model_width), jnp.float32)
    for tap_index in range(tap_count):
        conv_sum = conv_sum + conv_kernel[tap_index] * padded[:, tap_index : tap_index + frames_dev]
    middle_frames = middle_wide.reshape(recordings, frames_dev, model_width)
    block_out = (middle_frames + jax.nn.silu(conv_sum)).astype(jnp.bfloat16)
    upstream = cotangent.astype(jnp.float32)
    grad_conv_low = (upstream * silu_slope(conv_sum)).astype(jnp.bfloat16)
    grad_conv = lax.optimization_barrier(grad_conv_low).astype(jnp.float32)
    grad_padded = with_halo(grad_conv_low, (("ctx", 1),), rim_width).astype(jnp.float32)
    grad_input = jnp.zeros((recordings, frames_dev, model_width), jnp.float32)
    kernel_list = []
    for tap_index in range(tap_count):
        window = padded[:, tap_index : tap_index + frames_dev]
        kernel_list.append(jnp.sum(grad_conv * window, axis=(0, 1)))
        start_row = 2 * rim_width - tap_index
        grad_input = (
            grad_input + conv_kernel[tap_index] * grad_padded[:, start_row : start_row + frames_dev]
        )
    kernel_rows = jnp.stack(kernel_list)
    kernel_dp = lax.psum(kernel_rows, "dp")
    grad_middle = (
        upstream.reshape(-1, model_width)
        + norm_back(middle_wide, conv_inverse, conv_gain, grad_input.reshape(-1, model_width))
    ).astype(jnp.bfloat16)
    contract_rows = (((0,), (0,)), ((), ()))
    contract_columns = (((1,), (1,)), ((), ()))
    grad_mixed = lax.dot_general(
        grad_middle, weight_out, contract_columns, preferred_element_type=jnp.float32
    ).astype(jnp.bfloat16)
    mixed_columns = lax.all_to_all(mixed, "dp", split_axis=1, concat_axis=0, tiled=True)
    middle_rows = lax.all_gather(grad_middle, "dp", axis=0, tiled=True)
    grad_wout = lax.dot_general(
        mixed_columns, middle_rows, contract_rows, preferred_element_type=jnp.float32
    )
    grad_heads = grad_mixed.reshape(recordings, frames_dev, head_count, head_size)

    def backward_group(group):
        first_head = group * group_width
        queries = lax.dynamic_slice_in_dim(query_all, first_head, group_width, 2)
        key_part = lax.dynamic_slice_in_dim(key_all, first_head, group_width, 3)
        value_part = lax.dynamic_slice_in_dim(value_all, first_head, group_width, 3)
        grad_part = lax.dynamic_slice_in_dim(grad_heads, first_head, group_width, 2)
        probs = probabilities(queries, key_part, listed, score_scale)
        probs_low = probs.astype(jnp.bfloat16)
        key_flat = key_part.reshape(recordings, -1, group_width, head_size)
        value_flat = value_part.reshape(recordings, -1, group_width, head_size)
        grad_probs = jnp.einsum(
            "rqhd,rkhd->rhqk", grad_part, value_flat, preferred_element_type=jnp.float32
        )
        row_sum = jnp.sum(probs * grad_probs, axis=3, keepdims=True)
        grad_scores = (probs * (grad_probs - row_sum) * score_scale).astype(jnp.bfloat16)
        grad_query = jnp.einsum(
            "rhqk,rkhd->rqhd", grad_scores, key_flat, preferred_element_type=jnp.float32
        )
        grad_key = jnp.einsum(
            "rhqk,rqhd->rkhd", grad_scores, queries, preferred_element_type=jnp.float32
        )
        grad_value = jnp.einsum(
            "rhqk,rqhd->rkhd", probs_low, grad_part, preferred_element_type=jnp.float32
        )
        return (grad_query, grad_key, grad_value)

    grad_query, grad_key, grad_value = lax.map(
        backward_group, jnp.arange(group_count, dtype=jnp.int32)
    )
    grad_query = jnp.moveaxis(grad_query, 0, 2).reshape(recordings * frames_dev, model_width)
    grad_key = jnp.moveaxis(grad_key, 0, 2).reshape(recordings, seen_count, frames_dev, model_width)
    grad_value = jnp.moveaxis(grad_value, 0, 2).reshape(
        recordings, seen_count, frames_dev, model_width
    )
    pair_total = jnp.concatenate([grad_key[:, 0], grad_value[:, 0]], axis=2)
    for position, offset in enumerate(offsets):
        outgoing = jnp.concatenate(
            [grad_key[:, position + 1], grad_value[:, position + 1]], axis=2
        ).astype(jnp.bfloat16)
        arrived = from_behind(outgoing, "ctx", offset)
        pair_total = pair_total + arrived.astype(jnp.float32)
    grad_projected = jnp.concatenate(
        [
            grad_query.astype(jnp.bfloat16),
            pair_total.reshape(recordings * frames_dev, 2 * model_width).astype(jnp.bfloat16),
        ],
        axis=1,
    )
    normed_columns = lax.all_to_all(normed, "dp", split_axis=1, concat_axis=0, tiled=True)
    projected_rows = lax.all_gather(grad_projected, "dp", axis=0, tiled=True)
    grad_wqkv = lax.dot_general(
        normed_columns, projected_rows, contract_rows, preferred_element_type=jnp.float32
    )
    grad_normed = lax.dot_general(
        grad_projected, weight_qkv, contract_columns, preferred_element_type=jnp.float32
    )
    grad_embedded = (
        grad_middle.astype(jnp.float32) + norm_back(features, attn_inverse, attn_gain, grad_normed)
    ).astype(jnp.bfloat16)
    row_width = grad_wqkv.shape[1] + grad_wout.shape[1]
    kernel_padded = jnp.pad(
        kernel_dp, ((0, -tap_count * model_width % row_width // model_width), (0, 0))
    )
    kernel_packed = kernel_padded.reshape(-1, row_width)
    packed = jnp.concatenate(
        [jnp.concatenate([grad_wqkv, grad_wout], axis=1), kernel_packed], axis=0
    )
    summed = lax.psum(packed, "ctx")
    shard_rows = grad_wqkv.shape[0]
    grad_qkv = summed[:shard_rows, : grad_wqkv.shape[1]]
    grad_out = summed[:shard_rows, grad_wqkv.shape[1] :]
    grad_kernel = summed[shard_rows:].reshape(-1, model_width)[:tap_count]
    return (
        block_out,
        grad_embedded.reshape(recordings, frames_dev, model_width),
        grad_qkv,
        grad_out,
        grad_kernel,
    )


def solution(mesh):
    in_specs = (
        P("dp", "ctx", None),
        P(None, "dp", "ctx"),
        P("dp", None),
        P("dp", None),
        P(),
        P(),
        P(),
        P(),
        P(),
        P("dp", "ctx", None),
    )
    out_specs = (P("dp", "ctx", None), P("dp", "ctx", None), P("dp", None), P("dp", None), P())
    return jax.shard_map(
        on_device, mesh=mesh, in_specs=in_specs, out_specs=out_specs, check_vma=False
    )
```

profile of v0, /device:TPU:0, one launch (start us, length us, event | category | flops | bytes accessed | tf_op | source)
XLA Modules:
  0.0 895.1 jit_solution(8023950666195141221)
XLA Ops:
  9.8 24.0 %all_gather.19 = s32[1,4096,8]{1,2,0:T(8,128)S(1)} all-gather(s32[1,256,8]{1,2,0:T(8,128)} %param.16), channel_id=1, replica_groups=mesh['dp'=8,'ctx'=16] {'ctx'}, dimensions={1}, use_global_device_ids=true | all-gather | bytes 139264 | tf_op jit(solution)/shard_map/all_gather | solution.py:74
  34.5 3.7 all-gather.6.cloned.1.call-done
  39.8 12.1 %gather_fusion = bf16[4096,64]{1,0:T(8,128)(2,1)S(1)} fusion(bf16[1024,64]{1,0:T(8,128)(2,1)S(1)} %get-tuple-element.450, s32[4096]{0:T(1024)S(1)} %broadcast_clamp_fusion.7), kind=kCustom, calls=%fused_computation.clone | custom fusion | bytes 1064960 | tf_op jit(solution)/shard_map/jit(_take)/gather | solution.py:78
  52.0 15.0 %gather_fusion.7 = bf16[4096,64]{1,0:T(8,128)(2,1)} fusion(bf16[1024,64]{1,0:T(8,128)(2,1)S(1)} %get-tuple-element.451, s32[4096]{0:T(1024)S(1)} %broadcast_clamp_fusion), kind=kCustom, calls=%fused_computation.7.clone | custom fusion | bytes 1064960 | tf_op jit(solution)/shard_map/jit(_take)/gather | solution.py:78
  67.0 14.9 %gather_fusion.6 = bf16[4096,64]{1,0:T(8,128)(2,1)} fusion(bf16[1024,64]{1,0:T(8,128)(2,1)S(1)} %get-tuple-element.452, s32[4096]{0:T(1024)S(1)} %broadcast_clamp_fusion.1), kind=kCustom, calls=%fused_computation.6.clone | custom fusion | bytes 1064960 | tf_op jit(solution)/shard_map/jit(_take)/gather | solution.py:78
  81.9 14.9 %gather_fusion.5 = bf16[4096,64]{1,0:T(8,128)(2,1)} fusion(bf16[1024,64]{1,0:T(8,128)(2,1)S(1)} %get-tuple-element.453, s32[4096]{0:T(1024)S(1)} %broadcast_clamp_fusion.2), kind=kCustom, calls=%fused_computation.5.clone | custom fusion | bytes 1064960 | tf_op jit(solution)/shard_map/jit(_take)/gather | solution.py:78
  96.8 14.9 %gather_fusion.4 = bf16[4096,64]{1,0:T(8,128)(2,1)} fusion(bf16[1024,64]{1,0:T(8,128)(2,1)S(1)} %get-tuple-element.454, s32[4096]{0:T(1024)S(1)} %broadcast_clamp_fusion.3), kind=kCustom, calls=%fused_computation.4.clone | custom fusion | bytes 1064960 | tf_op jit(solution)/shard_map/jit(_take)/gather | solution.py:78
  111.7 14.9 %gather_fusion.3 = bf16[4096,64]{1,0:T(8,128)(2,1)} fusion(bf16[1024,64]{1,0:T(8,128)(2,1)S(1)} %get-tuple-element.455, s32[4096]{0:T(1024)S(1)} %broadcast_clamp_fusion.4), kind=kCustom, calls=%fused_computation.3.clone | custom fusion | bytes 1064960 | tf_op jit(solution)/shard_map/jit(_take)/gather | solution.py:78
  126.6 14.9 %gather_fusion.2 = bf16[4096,64]{1,0:T(8,128)(2,1)} fusion(bf16[1024,64]{1,0:T(8,128)(2,1)S(1)} %get-tuple-element.456, s32[4096]{0:T(1024)S(1)} %broadcast_clamp_fusion.5), kind=kCustom, calls=%fused_computation.2.clone | custom fusion | bytes 1064960 | tf_op jit(solution)/shard_map/jit(_take)/gather | solution.py:78
  141.5 14.9 %gather_fusion.1 = bf16[4096,64]{1,0:T(8,128)(2,1)} fusion(bf16[1024,64]{1,0:T(8,128)(2,1)S(1)} %get-tuple-element.457, s32[4096]{0:T(1024)S(1)} %broadcast_clamp_fusion.6), kind=kCustom, calls=%fused_computation.1.clone | custom fusion | bytes 1064960 | tf_op jit(solution)/shard_map/jit(_take)/gather | solution.py:78
  156.4 8.9 add_convert_fusion
  165.4 16.7 %copy.339 = bf16[1,4096,64]{2,0,1:T(2,128)(2,1)S(1)} copy(bf16[1,4096,64]{2,1,0:T(8,128)(2,1)S(1)} %add_convert_fusion) | data formatting | bytes 1048576 | tf_op jit(solution)/shard_map/convert_element_type | solution.py:82
  182.6 22.4 %reduce.51 = bf16[4096,64]{1,0:T(8,128)(2,1)S(1)} reduce(bf16[4096,1,64]{2,1,0:T(2,128)(2,1)S(1)} %bitcast.477, bf16[]{:T(256)} %broadcast.264), dimensions={1}, to_apply=%bitcast.392.reduce_sub_computation | reduce | bytes 1048578
  205.8 18.8 %all_to_all.44 = bf16[16,2,8192]{2,1,0:T(2,128)(2,1)S(1)} all-to-all(bf16[16,2,8192]{2,1,0:T(2,128)(2,1)S(1)} %reshape.933), channel_id=1, replica_groups=mesh['dp'=8,'ctx'=16] {'ctx'}, dimensions={0} | all-to-all | bytes 1048576 | tf_op jit(solution)/shard_map/all_to_all | solution.py:81
  230.3 4.6 fusion.102
  236.4 3.7 collective-permute-start.1
  240.1 3.5 collective-permute-start
  249.1 13.9 %collective-permute-done.1 = bf16[1,256,2048]{2,1,0:T(8,128)(2,1)} collective-permute-done((bf16[1,256,2048]{2,1,0:T(8,128)(2,1)}, bf16[1,256,2048]{2,1,0:T(8,128)(2,1)}, u32[]{:S(2)}, u32[]{:S(2)}) %collective-permute-start.1) | collective-permute-done | bytes 1048608 | tf_op jit(solution)/shard_map/ppermute | solution.py:14
  263.0 21.3 %collective-permute-done = bf16[1,256,2048]{2,1,0:T(8,128)(2,1)} collective-permute-done((bf16[1,256,2048]{2,1,0:T(8,128)(2,1)}, bf16[1,256,2048]{2,1,0:T(8,128)(2,1)}, u32[]{:S(2)}, u32[]{:S(2)}) %collective-permute-start) | collective-permute-done | bytes 1048608 | tf_op jit(solution)/shard_map/ppermute | solution.py:14
  288.9 4.0 copy.299
  292.8 3.9 copy.297
  296.7 4.8 copy.300
  301.5 46.3 %while.24 = (s32[]{:T(128)}, bf16[4,1,256,4,64]{2,4,3,1,0:T(8,128)(2,1)}, s32[4]{0:T(128)S(1)}, bf16[1,4,256,16,64]{2,1,4,3,0:T(4,128)(2,1)}, bf16[1,256,16,64]{...) while((s32[]{:T(128)}, ...), condition=%wide.region_10.12_spmd, body=%wide.region_4.11_spmd.sunk | while | flops 282916864 | bytes 16444675 | solution.py:129
  350.7 4.4 collective-permute-start.3
  357.0 4.0 collective-permute-done.4
  361.1 5.3 fusion.115
  369.0 3.3 collective-permute-start.5
  378.3 5.6 fusion.120
  388.2 143.3 %while.25 = (s32[]{:T(128)}, bf16[4,1,256,4,64]{2,4,3,1,0:T(8,128)(2,1)}, f32[4,1,1024,4,64]{2,4,3,1,0:T(8,128)}, f32[4,1,1024,4,64]{2,4,3,1,0:T(8,128)}, s32[4]...) while((s32[]{:T(128)}, ...), condition=%wide.region_20.22_spmd, body=%wide.region_13.21_spmd.sunk | while | flops 716965888 | bytes 66809192 | solution.py:203
  402.7 3.6 fusion.259
  406.4 7.0 fusion.265
  413.4 7.3 fusion.266
  420.7 3.1 fusion.267
  438.3 3.6 fusion.259
  442.0 7.0 fusion.265
  449.0 8.0 fusion.266
  457.0 3.2 fusion.267
  474.7 3.6 fusion.259
  478.4 7.0 fusion.265
  485.4 7.3 fusion.266
  492.7 3.2 fusion.267
  510.4 3.6 fusion.259
  514.0 7.0 fusion.265
  521.0 7.3 fusion.266
  528.3 3.1 fusion.267
  531.4 5.6 reshape.813
  542.1 5.8 reshape.812
  550.8 3.8 fusion.198
  554.6 3.6 copy.307
  564.9 3.6 copy.311
  568.5 3.6 copy.312
  574.6 7.6 pad_maximum_fusion.2
  583.5 7.3 pad_maximum_fusion.3
  590.8 5.5 collective-permute-start.9
  596.3 4.9 slice_bitcast_fusion
  601.4 35.3 %collective-permute-done.8 = bf16[1,256,2048]{1,0,2:T(2,128)(2,1)S(1)} collective-permute-done((bf16[1,256,2048]{1,0,2:T(2,128)(2,1)S(1)}, bf16[1,256,2048]{1,0,2:T(2,128)(2,1)S(1)}, u32[]{:S(2)}, u32[]{:S(2)}) %collective-permute-start.8) | collective-permute-done | bytes 1048608 | tf_op jit(solution)/shard_map/ppermute | solution.py:14
  638.7 19.2 %fusion.105 = bf16[1,256,2048]{1,0,2:T(2,128)(2,1)S(1)} fusion(bf16[1,256,2048]{1,0,2:T(2,128)(2,1)S(1)} %collective-permute-done.9, bf16[1,256,2048]{1,0,2:T(2,128)(2,1)S(1)} %collective-permute-done.8, f32[1,256,2048]{1,2,0:T(8,128)S(1)} %convert_element_type.227, f32[1,256,1024]{1,0,2:T(1,128)S(1)} %get-tuple-element.513, ...), kind=kLoop, calls=%fused_computation.149 | loop fusion | flops 3670016 | bytes 7340032 | tf_op jit(solution)/shard_map/convert_element_type | solution.py:221
  659.7 13.6 %all_to_all.45 = bf16[256,8,128]{0,2,1:T(8,128)(2,1)S(1)} all-to-all(bf16[256,8,128]{0,2,1:T(8,128)(2,1)S(1)} %multiply_convert_fusion.1), channel_id=1, replica_groups=mesh['dp'=8,'ctx'=16] {'dp'}, dimensions={1} | all-to-all | bytes 1048576 | tf_op jit(solution)/shard_map/all_to_all | solution.py:225
  673.2 3.5 all-to-all-start.2
  678.4 8.6 all-to-all-done.2
  690.3 83.4 %all-gather.12.cloned.1.call-done = bf16[2048,3072]{0,1:T(8,128)(2,1)} async-done(((bf16[256,3072]{0,1:T(8,128)(2,1)}), bf16[2048,3072]{0,1:T(8,128)(2,1)}) %all-gather.12.cloned.1.call-update) | async-done | bytes 12582928 | tf_op jit(solution)/shard_map/all_gather | solution.py:226
  773.7 8.9 fusion.203
  786.7 4.8 multiply_reduce_fusion.1
  792.7 88.8 %all-reduce.6.cloned.1.call-done = f32[136,4096]{1,0:T(8,128)} async-done(((f32[136,4096]{1,0:T(8,128)}), f32[136,4096]{1,0:T(8,128)}) %all-reduce.6.cloned.1.call-update) | async-done | bytes 2228240 | tf_op jit(solution)/shard_map/psum | solution.py:244
  (255 shorter events, 177.4 us)
Async XLA Ops:
  7.2 237.8 %copy-start = (s32[16,1]{0,1:T(1,128)S(1)}, s32[16,1]{0,1:T(1,128)}, u32[]{:S(2)}) copy-start(s32[16,1]{0,1:T(1,128)} %param.24) | copy-start | bytes 196
  7.2 31.0 %all-gather.6.cloned.1.call-start = ((), (), s32[]{:S(2)}) async-start(), calls=%async_computation.3 | async-start | bytes 2359296 | tf_op jit(solution)/shard_map/all_gather | solution.py:75
  9.0 220.7 %all-gather.8.cloned.1.call-start = ((), (), s32[]{:S(2)}) async-start(), calls=%async_computation.4 | async-start | bytes 7077888 | tf_op jit(solution)/shard_map/all_gather | solution.py:85
  9.8 338.1 %all-gather.10.cloned.1.call-start = ((), (), s32[]{:S(2)}) async-start(), calls=%async_computation.5 | async-start | bytes 2359296 | tf_op jit(solution)/shard_map/all_gather | solution.py:86
  141.5 14.9 %copy-start.12 = (bf16[4096,64]{1,0:T(8,128)(2,1)S(1)}, bf16[4096,64]{1,0:T(8,128)(2,1)}, u32[]{:S(2)}) copy-start(bf16[4096,64]{1,0:T(8,128)(2,1)} %gather_fusion.7) | copy-start | bytes 1572868
  228.1 2.2 copy-start.19
  229.2 5.7 copy-start.8
  229.6 118.3 %copy-start.6 = (f32[256,1024]{1,0:T(8,128)}, f32[256,1024]{1,0:T(8,128)S(1)}, u32[]{:S(2)}) copy-start(f32[256,1024]{1,0:T(8,128)S(1)} %copy.302) | copy-start | bytes 3145732
  229.6 0.6 copy-start.21
  229.6 16.6 %copy-start.23 = (s32[16,2]{0,1:T(2,128)S(1)}, s32[16,2]{0,1:T(2,128)}, u32[]{:S(2)}) copy-start(s32[16,2]{0,1:T(2,128)} %param.23) | copy-start | bytes 388
  229.7 17.3 %copy-start.17 = (f32[31,1024]{1,0:T(8,128)S(1)}, f32[31,1024]{1,0:T(8,128)}, u32[]{:S(2)}) copy-start(f32[31,1024]{1,0:T(8,128)} %param.22) | copy-start | bytes 380932
  234.9 1.5 copy-start.14
  236.4 26.6 %collective-permute-start.1 = (bf16[1,256,2048]{2,1,0:T(8,128)(2,1)}, bf16[1,256,2048]{2,1,0:T(8,128)(2,1)}, u32[]{:S(2)}, u32[]{:S(2)}) collective-permute-start(bf16[1,256,2048]{2,1,0:T(8,128)(2,1)} %get-tuple-element.459), channel_id=1, source_target_pairs={{0,2},{1,3},{2,4},{3,5},{4,6},{5,7},{6,8},{7,9},{8,10},{9,11},{10,... | collective-permute-start | bytes 3145736 | tf_op jit(solution)/shard_map/ppermute | solution.py:14
  240.1 44.2 %collective-permute-start = (bf16[1,256,2048]{2,1,0:T(8,128)(2,1)}, bf16[1,256,2048]{2,1,0:T(8,128)(2,1)}, u32[]{:S(2)}, u32[]{:S(2)}) collective-permute-start(bf16[1,256,2048]{2,1,0:T(8,128)(2,1)} %get-tuple-element.459), channel_id=1, source_target_pairs={{0,1},{1,2},{2,3},{3,4},{4,5},{5,6},{6,7},{7,8},{8,9},{9,10},{10,1... | collective-permute-start | bytes 3145736 | tf_op jit(solution)/shard_map/ppermute | solution.py:14
  243.6 40.7 %collective-permute-start.2 = (bf16[1,256,2048]{2,1,0:T(8,128)(2,1)}, bf16[1,256,2048]{2,1,0:T(8,128)(2,1)}, u32[]{:S(2)}, u32[]{:S(2)}) collective-permute-start(bf16[1,256,2048]{2,1,0:T(8,128)(2,1)} %get-tuple-element.459), channel_id=1, source_target_pairs={{1,0},{2,1},{3,2},{4,3},{5,4},{6,5},{7,6},{8,7},{9,8},{10,9},{11,1... | collective-permute-start | bytes 3145736 | tf_op jit(solution)/shard_map/ppermute | solution.py:14
  244.9 432.5 %all-reduce.4.cloned.1.call-start = ((), (), s32[]{:S(2)}) async-start(), calls=%async_computation.8 | async-start | bytes 262144 | tf_op jit(solution)/shard_map/psum | solution.py:160
  347.8 2.7 copy-start.18
  347.8 13.3 %copy-start.13 = (bf16[1,256,1024]{2,1,0:T(8,128)(2,1)S(1)}, bf16[1,256,1024]{2,1,0:T(8,128)(2,1)}, u32[]{:S(2)}) copy-start(bf16[1,256,1024]{2,1,0:T(8,128)(2,1)} %param.25) | copy-start | bytes 1572868
  350.5 33.4 %copy-start.4 = (bf16[256,1024]{1,0:T(8,128)(2,1)}, bf16[256,1024]{1,0:T(8,128)(2,1)S(1)}, u32[]{:S(2)}) copy-start(bf16[256,1024]{1,0:T(8,128)(2,1)S(1)} %get-tuple-element.510) | copy-start | bytes 1572868
  350.7 6.2 collective-permute-start.3
  355.2 5.8 collective-permute-start.4
  369.0 9.1 %collective-permute-start.5 = (bf16[1,15,1024]{2,1,0:T(8,128)(2,1)S(1)}, bf16[1,15,1024]{2,1,0:T(8,128)(2,1)S(1)}, u32[]{:S(2)}, u32[]{:S(2)}) collective-permute-start(bf16[1,15,1024]{2,1,0:T(8,128)(2,1)S(1)} %get-tuple-element.460), channel_id=1, source_target_pairs={{0,1},{1,2},{2,3},{3,4},{4,5},{5,6},{6,7},{7,8},{8,9},{9,10},{10,1... | collective-permute-start | bytes 92168 | tf_op jit(solution)/shard_map/ppermute | solution.py:22
  372.3 5.8 collective-permute-start.6
  378.1 309.3 %all-gather.14.cloned.1.call-start = ((), (), s32[]{:S(2)}) async-start(), calls=%async_computation.7 | async-start | bytes 4718592 | tf_op jit(solution)/shard_map/all_gather | solution.py:171
  384.4 3.6 copy-start.10
  388.0 385.7 %all-gather.12.cloned.1.call-start = ((), (), s32[]{:S(2)}) async-start(), calls=%async_computation.6 | async-start | bytes 14155776 | tf_op jit(solution)/shard_map/all_gather | solution.py:226
  396.4 6.3 copy-start.3
  401.1 1.0 copy-start.2
  432.1 6.3 copy-start.3
  436.8 1.0 copy-start.2
  468.4 6.3 copy-start.3
  473.1 1.0 copy-start.2
  504.1 6.3 copy-start.3
  508.8 1.0 copy-start.2
  573.3 27.9 %collective-permute-start.7 = (bf16[1,256,2048]{1,2,0:T(8,128)(2,1)S(1)}, bf16[1,256,2048]{1,2,0:T(8,128)(2,1)S(1)}, u32[]{:S(2)}, u32[]{:S(2)}) collective-permute-start(bf16[1,256,2048]{1,2,0:T(8,128)(2,1)S(1)} %pad_maximum_fusion.5), channel_id=1, source_target_pairs={{1,0},{2,1},{3,2},{4,3},{5,4},{6,5},{7,6},{8,7},{9,8},{10,9},{11,1... | collective-permute-start | bytes 3145736 | tf_op jit(solution)/shard_map/ppermute | solution.py:14
  582.2 54.5 %collective-permute-start.8 = (bf16[1,256,2048]{1,0,2:T(2,128)(2,1)S(1)}, bf16[1,256,2048]{1,0,2:T(2,128)(2,1)S(1)}, u32[]{:S(2)}, u32[]{:S(2)}) collective-permute-start(bf16[1,256,2048]{1,0,2:T(2,128)(2,1)S(1)} %pad_maximum_fusion.2), channel_id=1, source_target_pairs={{2,0},{3,1},{4,2},{5,3},{6,4},{7,5},{8,6},{9,7},{10,8},{11,9},{12,... | collective-permute-start | bytes 3145736 | tf_op jit(solution)/shard_map/ppermute | solution.py:14
  590.8 48.0 %collective-permute-start.9 = (bf16[1,256,2048]{1,0,2:T(2,128)(2,1)S(1)}, bf16[1,256,2048]{1,0,2:T(2,128)(2,1)S(1)}, u32[]{:S(2)}, u32[]{:S(2)}) collective-permute-start(bf16[1,256,2048]{1,0,2:T(2,128)(2,1)S(1)} %pad_maximum_fusion.3), channel_id=1, source_target_pairs={{0,1},{1,2},{2,3},{3,4},{4,5},{5,6},{6,7},{7,8},{8,9},{9,10},{10,1... | collective-permute-start | bytes 3145736 | tf_op jit(solution)/shard_map/ppermute | solution.py:14
  638.7 19.4 %copy-start.15 = (bf16[4,1,256,4,64]{2,4,3,1,0:T(8,128)(2,1)S(1)}, bf16[4,1,256,4,64]{2,4,3,1,0:T(8,128)(2,1)}, u32[]{:S(2)}) copy-start(bf16[4,1,256,4,64]{2,4,3,1,0:T(8,128)(2,1)} %get-tuple-element.118) | copy-start | bytes 1572868
  657.9 1.5 copy-start.9
  657.9 1.5 copy-start.20
  657.9 1.5 copy-start.22
  673.2 13.8 %all-to-all-start.2 = ((bf16[256,8,128]{0,2,1:T(8,128)(2,1)}), bf16[256,8,128]{0,2,1:T(8,128)(2,1)S(1)}, u32[]{:S(2)}, u32[]{:S(2)}) async-start(bf16[256,8,128]{0,2,1:T(8,128)(2,1)} %bitcast.135), calls=%async_computation.2 | async-start | bytes 1048576 | tf_op jit(solution)/shard_map/all_to_all | solution.py:170
  676.8 204.8 %all-reduce.6.cloned.1.call-start = ((), (), s32[]{:S(2)}) async-start(), calls=%async_computation.9 | async-start | bytes 4456448 | tf_op jit(solution)/shard_map/psum | solution.py:244
  782.6 1.6 copy-start.5
  782.7 4.0 copy-start.7
  784.2 2.5 copy-start.16
  786.7 4.8 copy-start.11
  786.7 101.0 %copy-start.1 = (s32[16,1]{0,1:T(1,128)S(1)}, s32[16,1]{0,1:T(1,128)}, u32[]{:S(2)}) copy-start(s32[16,1]{0,1:T(1,128)} %param.24) | copy-start | bytes 196
Sparse Core Ops, SparseCore 0:
  10.3 27.8 all-gather.5
  39.9 41.4 all-gather.7
  245.0 24.3 all-gather.9
  378.2 62.7 all-reduce.3
  442.6 31.2 all-gather.13
  659.6 114.0 all-gather.11
  784.4 97.1 all-reduce.5
where the time goes:
time: 906 us; the launch traced here: 895 us
  waiting for transfers between devices  262 us (29%)
  local copies, waits for them, and re-layouts  252 us (28%)
  matrix products  170 us (19%)
  other arithmetic  101 us (11%)
  blocking collectives  56.4 us (6%)
  starting transfers between devices  31.5 us (3%)
  between operations  16.1 us (2%)
    gather x8, local copies, waits for them, and re-layouts, on_device(): jnp.take(table_whole[codebook], ids_whole[:, :, codebook], axis=0)  117 us
    psum x1, waiting for transfers between devices, on_device(): summed = lax.psum(packed, 'ctx')  88.8 us
    all_gather x1, waiting for transfers between devices, on_device(): projected_rows = lax.all_gather(grad_projected, 'dp', axis=0, tiled=True)  83.4 us
    ppermute x6, waiting for transfers between devices, from_behind(): lax.ppermute(value, axis, [(source, source + steps) for source in range(f...  72.6 us
    dot_general x32, matrix products, block_scores(): jnp.einsum('rqhd,rkhd->rhqk', queries, key_block, preferred_element_type=...  52.1 us
    dot_general x4, matrix products, backward_group(): jnp.einsum('rhqk,rqhd->rkhd', grad_scores, queries, preferred_element_typ...  29.9 us
    dot_general x4, matrix products, backward_group(): jnp.einsum('rhqk,rkhd->rqhd', grad_scores, key_flat, preferred_element_ty...  28 us
    all_gather x1, blocking collectives, on_device(): ids_whole = lax.all_gather(ids, 'ctx', axis=1, tiled=True)  24 us
  transfers between devices with their start and end apart: 18, of which 9 were waited for; matrix products, arithmetic and copies ran while one was open for 54% of the time, Pallas kernels for 0%

commit v1 on v0

--- a/solution.py
+++ b/solution.py
@@ -241,7 +241,8 @@
     packed = jnp.concatenate(
         [jnp.concatenate([grad_wqkv, grad_wout], axis=1), kernel_packed], axis=0
     )
-    summed = lax.psum(packed, "ctx")
+    shards = lax.all_gather(packed, "ctx", axis=0, tiled=False)
+    summed = shards.sum(axis=0)
     shard_rows = grad_wqkv.shape[0]
     grad_qkv = summed[:shard_rows, : grad_wqkv.shape[1]]
     grad_out = summed[:shard_rows, grad_wqkv.shape[1] :]

time: 906 us -> 1030 us (1.14)
  waiting for transfers between devices: 262 us -> 379 us
  other arithmetic: 101 us -> 114 us
    all_gather x0 -> x1, waiting for transfers between devices: none -> 206 us  [on_device(): shards = lax.all_gather(packed, 'ctx', axis=0, tiled=False)]
    psum x1 -> x0, waiting for transfers between devices: 88.8 us -> none  [on_device(): summed = lax.psum(packed, 'ctx')]
    reduce_sum x0 -> x1, other arithmetic: none -> 13.2 us  [on_device(): summed = shards.sum(axis=0)]
  transfers between devices with their start and end apart: 18 -> 18, of which waited for: 9 -> 9; matrix products, arithmetic and copies ran while one was open for 54% -> 47% of each run, Pallas kernels for 0% -> 0%
where the time goes in v1:
time: 1030 us; the launch traced here: 1020 us
  waiting for transfers between devices  379 us (37%)
  local copies, waits for them, and re-layouts  249 us (24%)
  matrix products  171 us (17%)
  other arithmetic  114 us (11%)
  blocking collectives  56.3 us (5%)
  starting transfers between devices  31.5 us (3%)
  between operations  16.1 us (2%)
    all_gather x1, waiting for transfers between devices, on_device(): shards = lax.all_gather(packed, 'ctx', axis=0, tiled=False)  206 us
    gather x8, local copies, waits for them, and re-layouts, on_device(): jnp.take(table_whole[codebook], ids_whole[:, :, codebook], axis=0)  117 us
    all_gather x1, waiting for transfers between devices, on_device(): projected_rows = lax.all_gather(grad_projected, 'dp', axis=0, tiled=True)  83.3 us
    ppermute x6, waiting for transfers between devices, from_behind(): lax.ppermute(value, axis, [(source, source + steps) for source in range(f...  72.7 us
    dot_general x32, matrix products, block_scores(): jnp.einsum('rqhd,rkhd->rhqk', queries, key_block, preferred_element_type=...  52.2 us
    dot_general x4, matrix products, backward_group(): jnp.einsum('rhqk,rqhd->rkhd', grad_scores, queries, preferred_element_typ...  30.3 us
    dot_general x4, matrix products, backward_group(): jnp.einsum('rhqk,rkhd->rqhd', grad_scores, key_flat, preferred_element_ty...  28.4 us
    all_gather x1, blocking collectives, on_device(): ids_whole = lax.all_gather(ids, 'ctx', axis=1, tiled=True)  24 us
  transfers between devices with their start and end apart: 18, of which 9 were waited for; matrix products, arithmetic and copies ran while one was open for 47% of the time, Pallas kernels for 0%

profile of v1, /device:TPU:0, one launch (start us, length us, event | category | flops | bytes accessed | tf_op | source)
XLA Modules:
  0.0 1022.7 jit_solution(2993364734428720117)
XLA Ops:
  9.8 24.0 %all_gather.25 = s32[1,4096,8]{1,2,0:T(8,128)S(1)} all-gather(s32[1,256,8]{1,2,0:T(8,128)} %param.16), channel_id=1, replica_groups=mesh['dp'=8,'ctx'=16] {'ctx'}, dimensions={1}, use_global_device_ids=true | all-gather | bytes 139264 | tf_op jit(solution)/shard_map/all_gather | solution.py:74
  34.5 3.7 all-gather.8.cloned.1.call-done
  39.8 12.1 %gather_fusion = bf16[4096,64]{1,0:T(8,128)(2,1)S(1)} fusion(bf16[1024,64]{1,0:T(8,128)(2,1)S(1)} %get-tuple-element.450, s32[4096]{0:T(1024)S(1)} %broadcast_clamp_fusion.7), kind=kCustom, calls=%fused_computation.clone | custom fusion | bytes 1064960 | tf_op jit(solution)/shard_map/jit(_take)/gather | solution.py:78
  52.0 15.0 %gather_fusion.7 = bf16[4096,64]{1,0:T(8,128)(2,1)} fusion(bf16[1024,64]{1,0:T(8,128)(2,1)S(1)} %get-tuple-element.451, s32[4096]{0:T(1024)S(1)} %broadcast_clamp_fusion), kind=kCustom, calls=%fused_computation.7.clone | custom fusion | bytes 1064960 | tf_op jit(solution)/shard_map/jit(_take)/gather | solution.py:78
  67.0 14.9 %gather_fusion.6 = bf16[4096,64]{1,0:T(8,128)(2,1)} fusion(bf16[1024,64]{1,0:T(8,128)(2,1)S(1)} %get-tuple-element.452, s32[4096]{0:T(1024)S(1)} %broadcast_clamp_fusion.1), kind=kCustom, calls=%fused_computation.6.clone | custom fusion | bytes 1064960 | tf_op jit(solution)/shard_map/jit(_take)/gather | solution.py:78
  81.9 14.9 %gather_fusion.5 = bf16[4096,64]{1,0:T(8,128)(2,1)} fusion(bf16[1024,64]{1,0:T(8,128)(2,1)S(1)} %get-tuple-element.453, s32[4096]{0:T(1024)S(1)} %broadcast_clamp_fusion.2), kind=kCustom, calls=%fused_computation.5.clone | custom fusion | bytes 1064960 | tf_op jit(solution)/shard_map/jit(_take)/gather | solution.py:78
  96.8 14.9 %gather_fusion.4 = bf16[4096,64]{1,0:T(8,128)(2,1)} fusion(bf16[1024,64]{1,0:T(8,128)(2,1)S(1)} %get-tuple-element.454, s32[4096]{0:T(1024)S(1)} %broadcast_clamp_fusion.3), kind=kCustom, calls=%fused_computation.4.clone | custom fusion | bytes 1064960 | tf_op jit(solution)/shard_map/jit(_take)/gather | solution.py:78
  111.7 14.9 %gather_fusion.3 = bf16[4096,64]{1,0:T(8,128)(2,1)} fusion(bf16[1024,64]{1,0:T(8,128)(2,1)S(1)} %get-tuple-element.455, s32[4096]{0:T(1024)S(1)} %broadcast_clamp_fusion.4), kind=kCustom, calls=%fused_computation.3.clone | custom fusion | bytes 1064960 | tf_op jit(solution)/shard_map/jit(_take)/gather | solution.py:78
  126.6 14.9 %gather_fusion.2 = bf16[4096,64]{1,0:T(8,128)(2,1)} fusion(bf16[1024,64]{1,0:T(8,128)(2,1)S(1)} %get-tuple-element.456, s32[4096]{0:T(1024)S(1)} %broadcast_clamp_fusion.5), kind=kCustom, calls=%fused_computation.2.clone | custom fusion | bytes 1064960 | tf_op jit(solution)/shard_map/jit(_take)/gather | solution.py:78
  141.5 14.9 %gather_fusion.1 = bf16[4096,64]{1,0:T(8,128)(2,1)} fusion(bf16[1024,64]{1,0:T(8,128)(2,1)S(1)} %get-tuple-element.457, s32[4096]{0:T(1024)S(1)} %broadcast_clamp_fusion.6), kind=kCustom, calls=%fused_computation.1.clone | custom fusion | bytes 1064960 | tf_op jit(solution)/shard_map/jit(_take)/gather | solution.py:78
  156.4 8.9 add_convert_fusion
  165.4 16.7 %copy.339 = bf16[1,4096,64]{2,0,1:T(2,128)(2,1)S(1)} copy(bf16[1,4096,64]{2,1,0:T(8,128)(2,1)S(1)} %add_convert_fusion) | data formatting | bytes 1048576 | tf_op jit(solution)/shard_map/convert_element_type | solution.py:82
  182.6 22.4 %reduce.51 = bf16[4096,64]{1,0:T(8,128)(2,1)S(1)} reduce(bf16[4096,1,64]{2,1,0:T(2,128)(2,1)S(1)} %bitcast.479, bf16[]{:T(256)} %broadcast.264), dimensions={1}, to_apply=%bitcast.393.reduce_sub_computation | reduce | bytes 1048578
  205.8 18.8 %all_to_all.44 = bf16[16,2,8192]{2,1,0:T(2,128)(2,1)S(1)} all-to-all(bf16[16,2,8192]{2,1,0:T(2,128)(2,1)S(1)} %reshape.934), channel_id=1, replica_groups=mesh['dp'=8,'ctx'=16] {'ctx'}, dimensions={0} | all-to-all | bytes 1048576 | tf_op jit(solution)/shard_map/all_to_all | solution.py:81
  230.3 4.6 fusion.102
  236.4 3.7 collective-permute-start.1
  240.1 3.4 collective-permute-start
  249.1 13.9 %collective-permute-done.1 = bf16[1,256,2048]{2,1,0:T(8,128)(2,1)} collective-permute-done((bf16[1,256,2048]{2,1,0:T(8,128)(2,1)}, bf16[1,256,2048]{2,1,0:T(8,128)(2,1)}, u32[]{:S(2)}, u32[]{:S(2)}) %collective-permute-start.1) | collective-permute-done | bytes 1048608 | tf_op jit(solution)/shard_map/ppermute | solution.py:14
  263.0 21.3 %collective-permute-done = bf16[1,256,2048]{2,1,0:T(8,128)(2,1)} collective-permute-done((bf16[1,256,2048]{2,1,0:T(8,128)(2,1)}, bf16[1,256,2048]{2,1,0:T(8,128)(2,1)}, u32[]{:S(2)}, u32[]{:S(2)}) %collective-permute-start) | collective-permute-done | bytes 1048608 | tf_op jit(solution)/shard_map/ppermute | solution.py:14
  288.9 4.0 copy.299
  292.9 4.0 copy.297
  296.9 4.7 copy.300
  301.5 46.4 %while.24 = (s32[]{:T(128)}, bf16[4,1,256,4,64]{2,4,3,1,0:T(8,128)(2,1)}, s32[4]{0:T(128)S(1)}, bf16[1,4,256,16,64]{2,1,4,3,0:T(4,128)(2,1)}, bf16[1,256,16,64]{...) while((s32[]{:T(128)}, ...), condition=%wide.region_10.12_spmd, body=%wide.region_4.11_spmd.sunk | while | flops 282916864 | bytes 16444675 | solution.py:129
  350.8 4.4 collective-permute-start.3
  357.0 4.0 collective-permute-done.4
  361.2 5.2 fusion.115
  369.0 3.3 collective-permute-start.5
  378.4 5.6 fusion.120
  388.3 144.2 %while.25 = (s32[]{:T(128)}, bf16[4,1,256,4,64]{2,4,3,1,0:T(8,128)(2,1)}, f32[4,1,1024,4,64]{2,4,3,1,0:T(8,128)}, f32[4,1,1024,4,64]{2,4,3,1,0:T(8,128)}, s32[4]...) while((s32[]{:T(128)}, ...), condition=%wide.region_20.22_spmd, body=%wide.region_13.21_spmd.sunk | while | flops 716965888 | bytes 66809192 | solution.py:203
  402.8 3.6 fusion.259
  406.4 7.1 fusion.265
  413.6 7.5 fusion.266
  421.0 3.1 fusion.267
  438.7 3.6 fusion.259
  442.3 7.1 fusion.265
  449.4 8.0 fusion.266
  457.4 3.2 fusion.267
  475.2 3.6 fusion.259
  478.9 7.1 fusion.265
  486.0 7.4 fusion.266
  493.4 3.2 fusion.267
  511.1 3.6 fusion.259
  514.8 7.1 fusion.265
  521.8 7.5 fusion.266
  532.4 5.6 reshape.813
  543.1 5.8 reshape.812
  551.8 3.8 fusion.198
  555.6 3.5 copy.307
  565.8 3.5 copy.311
  569.3 3.6 copy.312
  575.5 7.6 pad_maximum_fusion.2
  584.3 7.3 pad_maximum_fusion.3
  591.6 5.5 collective-permute-start.9
  597.1 4.9 slice_bitcast_fusion
  602.2 35.2 %collective-permute-done.8 = bf16[1,256,2048]{1,0,2:T(2,128)(2,1)S(1)} collective-permute-done((bf16[1,256,2048]{1,0,2:T(2,128)(2,1)S(1)}, bf16[1,256,2048]{1,0,2:T(2,128)(2,1)S(1)}, u32[]{:S(2)}, u32[]{:S(2)}) %collective-permute-start.8) | collective-permute-done | bytes 1048608 | tf_op jit(solution)/shard_map/ppermute | solution.py:14
  639.6 19.2 %fusion.105 = bf16[1,256,2048]{1,0,2:T(2,128)(2,1)S(1)} fusion(bf16[1,256,2048]{1,0,2:T(2,128)(2,1)S(1)} %collective-permute-done.9, bf16[1,256,2048]{1,0,2:T(2,128)(2,1)S(1)} %collective-permute-done.8, f32[1,256,2048]{1,2,0:T(8,128)S(1)} %convert_element_type.227, f32[1,256,1024]{1,0,2:T(1,128)S(1)} %get-tuple-element.513, ...), kind=kLoop, calls=%fused_computation.149 | loop fusion | flops 3670016 | bytes 7340032 | tf_op jit(solution)/shard_map/convert_element_type | solution.py:221
  660.6 13.5 %all_to_all.45 = bf16[256,8,128]{0,2,1:T(8,128)(2,1)S(1)} all-to-all(bf16[256,8,128]{0,2,1:T(8,128)(2,1)S(1)} %multiply_convert_fusion.1), channel_id=1, replica_groups=mesh['dp'=8,'ctx'=16] {'dp'}, dimensions={1} | all-to-all | bytes 1048576 | tf_op jit(solution)/shard_map/all_to_all | solution.py:225
  674.1 3.5 all-to-all-start.2
  679.2 8.6 all-to-all-done.2
  691.1 83.3 %all-gather.14.cloned.1.call-done = bf16[2048,3072]{0,1:T(8,128)(2,1)} async-done(((bf16[256,3072]{0,1:T(8,128)(2,1)}), bf16[2048,3072]{0,1:T(8,128)(2,1)}) %all-gather.14.cloned.1.call-update) | async-done | bytes 12582928 | tf_op jit(solution)/shard_map/all_gather | solution.py:226
  774.4 8.9 fusion.203
  787.4 4.8 multiply_reduce_fusion.1
  793.5 205.8 %all-gather.18.cloned.1.call-done = f32[2176,4096]{1,0:T(8,128)} async-done(((f32[136,4096]{1,0:T(8,128)}), f32[2176,4096]{1,0:T(8,128)}) %all-gather.18.cloned.1.call-update) | async-done | bytes 35651600 | tf_op jit(solution)/shard_map/all_gather | solution.py:244
  999.3 13.2 %reduce_sum.395 = f32[136,4096]{1,0:T(8,128)S(1)} reduce(f32[16,136,4096]{2,1,0:T(8,128)} %bitcast.475, f32[]{:T(128)} %constant.63.clone.1), dimensions={0}, to_apply=%region_54.56 | reduce | flops 8355840 | bytes 37879812 | tf_op jit(solution)/shard_map/reduce_sum | solution.py:245
  (256 shorter events, 177.5 us)
Async XLA Ops:
  7.2 237.8 %copy-start = (s32[16,1]{0,1:T(1,128)S(1)}, s32[16,1]{0,1:T(1,128)}, u32[]{:S(2)}) copy-start(s32[16,1]{0,1:T(1,128)} %param.24) | copy-start | bytes 196
  7.2 31.0 %all-gather.8.cloned.1.call-start = ((), (), s32[]{:S(2)}) async-start(), calls=%async_computation.3 | async-start | bytes 2359296 | tf_op jit(solution)/shard_map/all_gather | solution.py:75
  9.0 220.7 %all-gather.10.cloned.1.call-start = ((), (), s32[]{:S(2)}) async-start(), calls=%async_computation.4 | async-start | bytes 7077888 | tf_op jit(solution)/shard_map/all_gather | solution.py:85
  9.8 338.2 %all-gather.12.cloned.1.call-start = ((), (), s32[]{:S(2)}) async-start(), calls=%async_computation.5 | async-start | bytes 2359296 | tf_op jit(solution)/shard_map/all_gather | solution.py:86
  141.5 14.9 %copy-start.12 = (bf16[4096,64]{1,0:T(8,128)(2,1)S(1)}, bf16[4096,64]{1,0:T(8,128)(2,1)}, u32[]{:S(2)}) copy-start(bf16[4096,64]{1,0:T(8,128)(2,1)} %gather_fusion.7) | copy-start | bytes 1572868
  228.1 2.2 copy-start.19
  229.2 5.7 copy-start.8
  229.6 118.3 %copy-start.6 = (f32[256,1024]{1,0:T(8,128)}, f32[256,1024]{1,0:T(8,128)S(1)}, u32[]{:S(2)}) copy-start(f32[256,1024]{1,0:T(8,128)S(1)} %copy.302) | copy-start | bytes 3145732
  229.6 0.6 copy-start.21
  229.6 16.6 %copy-start.23 = (s32[16,2]{0,1:T(2,128)S(1)}, s32[16,2]{0,1:T(2,128)}, u32[]{:S(2)}) copy-start(s32[16,2]{0,1:T(2,128)} %param.23) | copy-start | bytes 388
  229.7 17.3 %copy-start.17 = (f32[31,1024]{1,0:T(8,128)S(1)}, f32[31,1024]{1,0:T(8,128)}, u32[]{:S(2)}) copy-start(f32[31,1024]{1,0:T(8,128)} %param.22) | copy-start | bytes 380932
  234.9 1.5 copy-start.14
  236.4 26.6 %collective-permute-start.1 = (bf16[1,256,2048]{2,1,0:T(8,128)(2,1)}, bf16[1,256,2048]{2,1,0:T(8,128)(2,1)}, u32[]{:S(2)}, u32[]{:S(2)}) collective-permute-start(bf16[1,256,2048]{2,1,0:T(8,128)(2,1)} %get-tuple-element.459), channel_id=1, source_target_pairs={{0,2},{1,3},{2,4},{3,5},{4,6},{5,7},{6,8},{7,9},{8,10},{9,11},{10,... | collective-permute-start | bytes 3145736 | tf_op jit(solution)/shard_map/ppermute | solution.py:14
  240.1 44.2 %collective-permute-start = (bf16[1,256,2048]{2,1,0:T(8,128)(2,1)}, bf16[1,256,2048]{2,1,0:T(8,128)(2,1)}, u32[]{:S(2)}, u32[]{:S(2)}) collective-permute-start(bf16[1,256,2048]{2,1,0:T(8,128)(2,1)} %get-tuple-element.459), channel_id=1, source_target_pairs={{0,1},{1,2},{2,3},{3,4},{4,5},{5,6},{6,7},{7,8},{8,9},{9,10},{10,1... | collective-permute-start | bytes 3145736 | tf_op jit(solution)/shard_map/ppermute | solution.py:14
  243.6 40.7 %collective-permute-start.2 = (bf16[1,256,2048]{2,1,0:T(8,128)(2,1)}, bf16[1,256,2048]{2,1,0:T(8,128)(2,1)}, u32[]{:S(2)}, u32[]{:S(2)}) collective-permute-start(bf16[1,256,2048]{2,1,0:T(8,128)(2,1)} %get-tuple-element.459), channel_id=1, source_target_pairs={{1,0},{2,1},{3,2},{4,3},{5,4},{6,5},{7,6},{8,7},{9,8},{10,9},{11,1... | collective-permute-start | bytes 3145736 | tf_op jit(solution)/shard_map/ppermute | solution.py:14
  244.9 433.3 %all-reduce.3.cloned.1.call-start = ((), (), s32[]{:S(2)}) async-start(), calls=%async_computation.8 | async-start | bytes 262144 | tf_op jit(solution)/shard_map/psum | solution.py:160
  347.9 2.7 copy-start.18
  347.9 13.3 %copy-start.13 = (bf16[1,256,1024]{2,1,0:T(8,128)(2,1)S(1)}, bf16[1,256,1024]{2,1,0:T(8,128)(2,1)}, u32[]{:S(2)}) copy-start(bf16[1,256,1024]{2,1,0:T(8,128)(2,1)} %param.25) | copy-start | bytes 1572868
  350.6 33.4 %copy-start.4 = (bf16[256,1024]{1,0:T(8,128)(2,1)}, bf16[256,1024]{1,0:T(8,128)(2,1)S(1)}, u32[]{:S(2)}) copy-start(bf16[256,1024]{1,0:T(8,128)(2,1)S(1)} %get-tuple-element.510) | copy-start | bytes 1572868
  350.8 6.2 collective-permute-start.3
  355.2 5.8 collective-permute-start.4
  369.0 9.2 collective-permute-start.5
  372.3 5.8 collective-permute-start.6
  378.1 310.0 %all-gather.16.cloned.1.call-start = ((), (), s32[]{:S(2)}) async-start(), calls=%async_computation.7 | async-start | bytes 4718592 | tf_op jit(solution)/shard_map/all_gather | solution.py:171
  384.5 3.5 copy-start.10
  388.0 386.4 %all-gather.14.cloned.1.call-start = ((), (), s32[]{:S(2)}) async-start(), calls=%async_computation.6 | async-start | bytes 14155776 | tf_op jit(solution)/shard_map/all_gather | solution.py:226
  396.5 6.3 copy-start.3
  401.2 1.0 copy-start.2
  432.4 6.3 copy-start.3
  437.1 1.0 copy-start.2
  469.0 6.3 copy-start.3
  473.7 1.0 copy-start.2
  504.8 6.3 copy-start.3
  509.5 1.0 copy-start.2
  574.2 27.9 %collective-permute-start.7 = (bf16[1,256,2048]{1,2,0:T(8,128)(2,1)S(1)}, bf16[1,256,2048]{1,2,0:T(8,128)(2,1)S(1)}, u32[]{:S(2)}, u32[]{:S(2)}) collective-permute-start(bf16[1,256,2048]{1,2,0:T(8,128)(2,1)S(1)} %pad_maximum_fusion.5), channel_id=1, source_target_pairs={{1,0},{2,1},{3,2},{4,3},{5,4},{6,5},{7,6},{8,7},{9,8},{10,9},{11,1... | collective-permute-start | bytes 3145736 | tf_op jit(solution)/shard_map/ppermute | solution.py:14
  583.0 54.3 %collective-permute-start.8 = (bf16[1,256,2048]{1,0,2:T(2,128)(2,1)S(1)}, bf16[1,256,2048]{1,0,2:T(2,128)(2,1)S(1)}, u32[]{:S(2)}, u32[]{:S(2)}) collective-permute-start(bf16[1,256,2048]{1,0,2:T(2,128)(2,1)S(1)} %pad_maximum_fusion.2), channel_id=1, source_target_pairs={{2,0},{3,1},{4,2},{5,3},{6,4},{7,5},{8,6},{9,7},{10,8},{11,9},{12,... | collective-permute-start | bytes 3145736 | tf_op jit(solution)/shard_map/ppermute | solution.py:14
  591.6 48.0 %collective-permute-start.9 = (bf16[1,256,2048]{1,0,2:T(2,128)(2,1)S(1)}, bf16[1,256,2048]{1,0,2:T(2,128)(2,1)S(1)}, u32[]{:S(2)}, u32[]{:S(2)}) collective-permute-start(bf16[1,256,2048]{1,0,2:T(2,128)(2,1)S(1)} %pad_maximum_fusion.3), channel_id=1, source_target_pairs={{0,1},{1,2},{2,3},{3,4},{4,5},{5,6},{6,7},{7,8},{8,9},{9,10},{10,1... | collective-permute-start | bytes 3145736 | tf_op jit(solution)/shard_map/ppermute | solution.py:14
  639.6 19.4 %copy-start.15 = (bf16[4,1,256,4,64]{2,4,3,1,0:T(8,128)(2,1)S(1)}, bf16[4,1,256,4,64]{2,4,3,1,0:T(8,128)(2,1)}, u32[]{:S(2)}) copy-start(bf16[4,1,256,4,64]{2,4,3,1,0:T(8,128)(2,1)} %get-tuple-element.118) | copy-start | bytes 1572868
  658.8 1.5 copy-start.9
  658.8 1.5 copy-start.20
  658.8 1.5 copy-start.22
  674.1 13.8 %all-to-all-start.2 = ((bf16[256,8,128]{0,2,1:T(8,128)(2,1)}), bf16[256,8,128]{0,2,1:T(8,128)(2,1)S(1)}, u32[]{:S(2)}, u32[]{:S(2)}) async-start(bf16[256,8,128]{0,2,1:T(8,128)(2,1)} %bitcast.135), calls=%async_computation.2 | async-start | bytes 1048576 | tf_op jit(solution)/shard_map/all_to_all | solution.py:170
  677.6 321.8 %all-gather.18.cloned.1.call-start = ((), (), s32[]{:S(2)}) async-start(), calls=%async_computation.9 | async-start | bytes 37879808 | tf_op jit(solution)/shard_map/all_gather | solution.py:244
  783.4 1.6 copy-start.5
  783.4 4.1 copy-start.7
  785.0 2.5 copy-start.16
  787.4 4.8 copy-start.11
  999.3 16.0 %copy-start.1 = (s32[16,1]{0,1:T(1,128)S(1)}, s32[16,1]{0,1:T(1,128)}, u32[]{:S(2)}) copy-start(s32[16,1]{0,1:T(1,128)} %param.24) | copy-start | bytes 196
Sparse Core Ops, SparseCore 0:
  10.3 27.8 all-gather.7
  39.9 41.4 all-gather.9
  245.0 24.3 all-gather.11
  378.2 62.7 all-reduce.2
  442.7 31.2 all-gather.15
  660.5 113.9 all-gather.13
  785.1 214.1 all-gather.17
